TPU v7x, 512 devices: a whole 4x8x8 slice. The times are simulated.
512 devices in a mesh: tm: 64 (over y, x, core), head: 8 (over z).
Axes of the slice: x: 4, y: 8, z: 8, core: 2. Of those that a mesh axis runs over, the one named last changes fastest.
Arguments:
- queries: bfloat16 [24576, 5120], P('tm', 'head')
- keys: bfloat16 [24576, 5120], P('tm', 'head')
- values: bfloat16 [24576, 5120], P('tm', 'head')
- text_keys: bfloat16 [512, 5120], P('tm', 'head'), may hold values from -6 to 6
- text_values: bfloat16 [512, 5120], P('tm', 'head')
- out_weight: bfloat16 [5120, 5120], P('head', 'tm'), may hold values from -0.25 to 0.25
- windows: int32 [64], replicated, may hold values from 0 to 4, as said below
- lengths: int32 [64], replicated, may hold values from 96 to 384, as said below
Outputs:
- mixed: bfloat16 [24576, 5120], P('tm', 'head')
Inputs may be any that keep to these rules, and one draw needn't show every extreme that they name: windows reach 4 for some frame in every draw. `lengths`: some frame is full in every draw.
All inputs are finite; a program needn't handle non-finite values.
Results may differ from a plain program's by a relative error of at most 0.014.
Values may be sent and summed in bfloat16 or wider, within the bound.
No kernel may reach another device: no remote copies, remote signals or barrier semaphores. Data moves between devices by JAX's collectives and lax.ppermute only.
A program may use at most 64 MiB of HBM per device.

v0:
```python
import math
import jax
import jax.numpy as jnp
from jax import lax
from jax.sharding import PartitionSpec as P

HD = 128
WIN = 4


def from_behind(value, axis, steps):
    count = lax.axis_size(axis)
    initial, last = (max(0, -steps), min(count, count - steps))
    return lax.ppermute(value, axis, [(source, source + steps) for source in range(initial, last)])


def on_device(queries, keys, values, text_keys, text_values, out_weight, windows, lengths):
    rows = queries.shape[0]
    width = queries.shape[1]
    local_heads = width // HD
    scale = 1.0 / math.sqrt(HD)
    position = lax.axis_index("tm")
    text_k, text_v = (
        lax.all_gather(text_keys, "tm", axis=0, tiled=True),
        lax.all_gather(text_values, "tm", axis=0, tiled=True),
    )
    key_list = [keys]
    value_list = [values]
    for step in range(1, WIN + 1):
        moved_k, moved_v = from_behind((keys, values), "tm", step)
        key_list.append(moved_k)
        value_list.append(moved_v)
    token_ids = jnp.arange(rows, dtype=jnp.int32)
    own_window = windows[position]
    mask_list = []
    for step in range(WIN + 1):
        source = position - step
        usable = (step <= own_window) & (source >= 0)
        source_len = lengths[jnp.maximum(source, 0)]
        mask_list.append(usable & (token_ids < source_len))
    mask_list.append(jnp.ones((text_k.shape[0],), bool))
    key_mask = jnp.concatenate(mask_list)
    all_keys = jnp.concatenate(key_list + [text_k], axis=0)
    all_values = jnp.concatenate(value_list + [text_v], axis=0)
    head_outputs = []
    for head_index in range(local_heads):
        lower = head_index * HD
        query_h = queries[:, lower : lower + HD]
        key_h = all_keys[:, lower : lower + HD]
        value_h = all_values[:, lower : lower + HD]
        scores = (
            lax.dot_general(
                query_h, key_h, (((1,), (1,)), ((), ())), preferred_element_type=jnp.float32
            )
            * scale
        )
        scores = jnp.where(key_mask[None, :], scores, -jnp.inf)
        top = jnp.max(scores, axis=-1, keepdims=True)
        weights = jnp.exp(scores - top)
        total = jnp.sum(weights, axis=-1, keepdims=True)
        attended = (
            jnp.dot(weights.astype(jnp.bfloat16), value_h, preferred_element_type=jnp.float32)
            / total
        )
        head_outputs.append(attended.astype(jnp.bfloat16))
    attended_all = jnp.concatenate(head_outputs, axis=1)
    partial_out = jnp.dot(
        attended_all,
        lax.all_gather(out_weight, "tm", axis=1, tiled=True),
        preferred_element_type=jnp.float32,
    )
    return lax.psum_scatter(
        partial_out.astype(jnp.bfloat16), "head", scatter_dimension=1, tiled=True
    )


def solution(mesh):
    return jax.shard_map(
        on_device,
        mesh=mesh,
        in_specs=(
            P("tm", "head"),
            P("tm", "head"),
            P("tm", "head"),
            P("tm", "head"),
            P("tm", "head"),
            P("head", "tm"),
            P(),
            P(),
        ),
        out_specs=P("tm", "head"),
        check_vma=False,
    )
```

profile of v0, /device:TPU:1, one launch (start us, length us, event | category | flops | bytes accessed | tf_op | source)
XLA Modules:
  0.0 300.5 jit_solution(977108429921644657)
XLA Ops:
  6.5 0.7 all-gather.2.cloned.1.call-update
  7.3 0.0 reduce-scatter.4.cloned.1.call-start
  7.3 4.5 %collective-permute-start = (bf16[384,640]{1,0:T(8,128)(2,1)}, bf16[384,640]{1,0:T(8,128)(2,1)S(1)}, u32[]{:S(2)}, u32[]{:S(2)}) collective-permute-start(bf16[384,640]{1,0:T(8,128)(2,1)} %param.9), channel_id=1, source_target_pairs={{0,8},{8,16},{16,24},{24,32},{32,40},{40,48},{48,56},{56,64},{64,7... | collective-permute-start | bytes 1474568 | tf_op jit(solution)/shard_map/ppermute | solution.py:14
  11.8 3.1 %collective-permute-start.1 = (bf16[384,640]{1,0:T(8,128)(2,1)}, bf16[384,640]{1,0:T(8,128)(2,1)S(1)}, u32[]{:S(2)}, u32[]{:S(2)}) collective-permute-start(bf16[384,640]{1,0:T(8,128)(2,1)} %param.9), channel_id=1, source_target_pairs={{0,16},{8,24},{16,32},{24,40},{32,48},{40,56},{48,64},{56,72},{64,... | collective-permute-start | bytes 1474568 | tf_op jit(solution)/shard_map/ppermute | solution.py:14
  15.0 3.4 %collective-permute-start.2 = (bf16[384,640]{1,0:T(8,128)(2,1)}, bf16[384,640]{1,0:T(8,128)(2,1)S(1)}, u32[]{:S(2)}, u32[]{:S(2)}) collective-permute-start(bf16[384,640]{1,0:T(8,128)(2,1)} %param.9), channel_id=1, source_target_pairs={{0,24},{8,32},{16,40},{24,48},{32,56},{40,64},{48,72},{56,80},{64,... | collective-permute-start | bytes 1474568 | tf_op jit(solution)/shard_map/ppermute | solution.py:14
  18.4 3.4 %collective-permute-start.3 = (bf16[384,640]{1,0:T(8,128)(2,1)}, bf16[384,640]{1,0:T(8,128)(2,1)S(1)}, u32[]{:S(2)}, u32[]{:S(2)}) collective-permute-start(bf16[384,640]{1,0:T(8,128)(2,1)} %param.9), channel_id=1, source_target_pairs={{0,32},{8,40},{16,48},{24,56},{32,64},{40,72},{48,80},{56,88},{64,... | collective-permute-start | bytes 1474568 | tf_op jit(solution)/shard_map/ppermute | solution.py:14
  21.9 3.7 %collective-permute-start.4 = (bf16[384,640]{1,0:T(8,128)(2,1)}, bf16[384,640]{1,0:T(8,128)(2,1)S(1)}, u32[]{:S(2)}, u32[]{:S(2)}) collective-permute-start(bf16[384,640]{1,0:T(8,128)(2,1)} %param.10), channel_id=1, source_target_pairs={{0,8},{8,16},{16,24},{24,32},{32,40},{40,48},{48,56},{56,64},{64,7... | collective-permute-start | bytes 1474568 | tf_op jit(solution)/shard_map/ppermute | solution.py:14
  25.6 1.2 dynamic_slice.18
  30.1 1.5 fusion.95
  31.6 0.6 fusion.90
  32.2 0.3 dynamic-update-slice.17
  32.4 0.6 fusion.91
  33.1 0.3 dynamic-update-slice.18
  33.3 0.6 fusion.92
  34.0 0.3 dynamic-update-slice.19
  34.2 0.6 fusion.93
  34.9 0.3 dynamic-update-slice.20
  35.1 0.7 fusion.94
  35.8 0.3 dynamic-update-slice.21
  36.0 0.2 dynamic-update-slice.22
  36.3 74.3 %all_gather.9 = bf16[512,640]{1,0:T(8,128)(2,1)S(1)} all-gather(bf16[8,640]{1,0:T(8,128)(2,1)} %param.11), channel_id=1, replica_groups=mesh['tm'=64,'head'=8] {'tm'}, dimensions={0}, use_global_device_ids=true | all-gather | bytes 665600 | tf_op jit(solution)/shard_map/all_gather | solution.py:24
  110.6 48.6 %all_gather.10 = bf16[512,640]{1,0:T(8,128)(2,1)S(1)} all-gather(bf16[8,640]{1,0:T(8,128)(2,1)} %param.12), channel_id=1, replica_groups=mesh['tm'=64,'head'=8] {'tm'}, dimensions={0}, use_global_device_ids=true | all-gather | bytes 665600 | tf_op jit(solution)/shard_map/all_gather | solution.py:25
  159.3 1.1 constant_dynamic-update-slice_fusion.5
  160.3 1.1 constant_dynamic-update-slice_fusion.11
  161.4 2.3 collective-permute-start.5
  163.7 0.1 constant_dynamic-update-slice_fusion.4
  163.8 0.0 collective-permute-done.1
  163.8 4.6 %collective-permute-start.6 = (bf16[384,640]{1,0:T(8,128)(2,1)S(1)}, bf16[384,640]{1,0:T(8,128)(2,1)S(1)}, u32[]{:S(2)}, u32[]{:S(2)}) collective-permute-start(bf16[384,640]{1,0:T(8,128)(2,1)S(1)} %copy-done), channel_id=1, source_target_pairs={{0,24},{8,32},{16,40},{24,48},{32,56},{40,64},{48,72},{56,80},{64,... | collective-permute-start | bytes 1474568 | tf_op jit(solution)/shard_map/ppermute | solution.py:14
  168.5 0.1 constant_dynamic-update-slice_fusion.3
  168.6 0.0 collective-permute-done.2
  168.6 2.3 collective-permute-start.7
  170.9 0.1 constant_dynamic-update-slice_fusion.2
  170.9 0.0 copy-start.1
  170.9 0.1 constant_dynamic-update-slice_fusion.1
  171.0 0.1 constant_dynamic-update-slice_fusion.10
  171.1 3.4 %collective-permute-done.5 = bf16[384,640]{1,0:T(8,128)(2,1)S(1)} collective-permute-done((bf16[384,640]{1,0:T(8,128)(2,1)}, bf16[384,640]{1,0:T(8,128)(2,1)S(1)}, u32[]{:S(2)}, u32[]{:S(2)}) %collective-permute-start.5) | collective-permute-done | bytes 491552 | tf_op jit(solution)/shard_map/ppermute | solution.py:14
  174.5 0.1 constant_dynamic-update-slice_fusion.9
  174.5 10.4 %collective-permute-done.6 = bf16[384,640]{1,0:T(8,128)(2,1)S(1)} collective-permute-done((bf16[384,640]{1,0:T(8,128)(2,1)S(1)}, bf16[384,640]{1,0:T(8,128)(2,1)S(1)}, u32[]{:S(2)}, u32[]{:S(2)}) %collective-permute-start.6) | collective-permute-done | bytes 491552 | tf_op jit(solution)/shard_map/ppermute | solution.py:14
  184.9 0.1 constant_dynamic-update-slice_fusion.8
  185.0 10.5 %collective-permute-done.7 = bf16[384,640]{1,0:T(8,128)(2,1)S(1)} collective-permute-done((bf16[384,640]{1,0:T(8,128)(2,1)S(1)}, bf16[384,640]{1,0:T(8,128)(2,1)S(1)}, u32[]{:S(2)}, u32[]{:S(2)}) %collective-permute-start.7) | collective-permute-done | bytes 491552 | tf_op jit(solution)/shard_map/ppermute | solution.py:14
  195.4 0.1 constant_dynamic-update-slice_fusion.7
  195.5 0.1 constant_dynamic-update-slice_fusion
  195.6 0.1 constant_dynamic-update-slice_fusion.6
  195.7 0.9 fusion.96
  196.6 0.6 fusion.5
  197.3 0.9 fusion.97
  198.1 0.6 fusion.7
  198.8 0.9 fusion.98
  199.7 0.6 fusion.9
  200.3 0.9 fusion.99
  201.2 0.6 fusion.11
  201.8 0.9 fusion.100
  202.7 0.6 fusion.13
  203.4 0.7 fusion.72
  204.1 0.7 fusion.66
  204.8 0.8 fusion.60
  205.6 0.7 fusion.54
  206.4 0.7 fusion.48
  207.1 0.0 all-gather.2.cloned.1.call-done
  207.1 8.9 %convolution_convert_fusion = bf16[384,5120]{1,0:T(8,128)(2,1)} fusion(bf16[384,640]{1,0:T(8,128)(2,1)S(1)} %fusion.48, bf16[640,5120]{0,1:T(8,128)(2,1)} %all-gather.2.cloned.1.call-done), kind=kOutput, calls=%fused_computation | convolution fusion | flops 2518548480 | bytes 10977280 | tf_op jit(solution)/shard_map/dot_general | solution.py:67
  216.1 6.3 %copy.9 = bf16[384,5120]{0,1:T(8,128)(2,1)} copy(bf16[384,5120]{1,0:T(8,128)(2,1)} %convolution_convert_fusion) | data formatting | bytes 7864320
  222.3 0.0 reduce-scatter.4.cloned.1.call-update
  222.4 69.3 %reduce-scatter.4.cloned.1.call-done = bf16[640,384]{1,0:T(8,128)(2,1)} async-done(((bf16[5120,384]{1,0:T(8,128)(2,1)}), bf16[640,384]{1,0:T(8,128)(2,1)}) %reduce-scatter.4.cloned.1.call-update) | async-done | bytes 491536
  291.6 2.0 copy.10
  (9 shorter events, 0.0 us)
Async XLA Ops:
  6.5 157.3 %copy-start = (bf16[384,640]{1,0:T(8,128)(2,1)S(1)}, bf16[384,640]{1,0:T(8,128)(2,1)}, u32[]{:S(2)}) copy-start(bf16[384,640]{1,0:T(8,128)(2,1)} %param.10) | copy-start | bytes 1474564
  6.5 200.6 %all-gather.2.cloned.1.call-start = ((), (), s32[]{:S(2)}) async-start(), calls=%async_computation.1 | async-start | bytes 6656000 | tf_op jit(solution)/shard_map/all_gather | solution.py:69
  7.3 284.4 %reduce-scatter.4.cloned.1.call-start = ((), (), s32[]{:S(2)}) async-start(), calls=%async_computation.2 | async-start | bytes 4423680
  7.3 154.1 %collective-permute-start = (bf16[384,640]{1,0:T(8,128)(2,1)}, bf16[384,640]{1,0:T(8,128)(2,1)S(1)}, u32[]{:S(2)}, u32[]{:S(2)}) collective-permute-start(bf16[384,640]{1,0:T(8,128)(2,1)} %param.9), channel_id=1, source_target_pairs={{0,8},{8,16},{16,24},{24,32},{32,40},{40,48},{48,56},{56,64},{64,7... | collective-permute-start | bytes 1474568 | tf_op jit(solution)/shard_map/ppermute | solution.py:14
  11.8 152.0 %collective-permute-start.1 = (bf16[384,640]{1,0:T(8,128)(2,1)}, bf16[384,640]{1,0:T(8,128)(2,1)S(1)}, u32[]{:S(2)}, u32[]{:S(2)}) collective-permute-start(bf16[384,640]{1,0:T(8,128)(2,1)} %param.9), channel_id=1, source_target_pairs={{0,16},{8,24},{16,32},{24,40},{32,48},{40,56},{48,64},{56,72},{64,... | collective-permute-start | bytes 1474568 | tf_op jit(solution)/shard_map/ppermute | solution.py:14
  15.0 153.6 %collective-permute-start.2 = (bf16[384,640]{1,0:T(8,128)(2,1)}, bf16[384,640]{1,0:T(8,128)(2,1)S(1)}, u32[]{:S(2)}, u32[]{:S(2)}) collective-permute-start(bf16[384,640]{1,0:T(8,128)(2,1)} %param.9), channel_id=1, source_target_pairs={{0,24},{8,32},{16,40},{24,48},{32,56},{40,64},{48,72},{56,80},{64,... | collective-permute-start | bytes 1474568 | tf_op jit(solution)/shard_map/ppermute | solution.py:14
  18.4 152.5 %collective-permute-start.3 = (bf16[384,640]{1,0:T(8,128)(2,1)}, bf16[384,640]{1,0:T(8,128)(2,1)S(1)}, u32[]{:S(2)}, u32[]{:S(2)}) collective-permute-start(bf16[384,640]{1,0:T(8,128)(2,1)} %param.9), channel_id=1, source_target_pairs={{0,32},{8,40},{16,48},{24,56},{32,64},{40,72},{48,80},{56,88},{64,... | collective-permute-start | bytes 1474568 | tf_op jit(solution)/shard_map/ppermute | solution.py:14
  21.9 149.1 %collective-permute-start.4 = (bf16[384,640]{1,0:T(8,128)(2,1)}, bf16[384,640]{1,0:T(8,128)(2,1)S(1)}, u32[]{:S(2)}, u32[]{:S(2)}) collective-permute-start(bf16[384,640]{1,0:T(8,128)(2,1)} %param.10), channel_id=1, source_target_pairs={{0,8},{8,16},{16,24},{24,32},{32,40},{40,48},{48,56},{56,64},{64,7... | collective-permute-start | bytes 1474568 | tf_op jit(solution)/shard_map/ppermute | solution.py:14
  161.4 13.1 %collective-permute-start.5 = (bf16[384,640]{1,0:T(8,128)(2,1)}, bf16[384,640]{1,0:T(8,128)(2,1)S(1)}, u32[]{:S(2)}, u32[]{:S(2)}) collective-permute-start(bf16[384,640]{1,0:T(8,128)(2,1)} %param.10), channel_id=1, source_target_pairs={{0,16},{8,24},{16,32},{24,40},{32,48},{40,56},{48,64},{56,72},{64,... | collective-permute-start | bytes 1474568 | tf_op jit(solution)/shard_map/ppermute | solution.py:14
  163.8 21.1 %collective-permute-start.6 = (bf16[384,640]{1,0:T(8,128)(2,1)S(1)}, bf16[384,640]{1,0:T(8,128)(2,1)S(1)}, u32[]{:S(2)}, u32[]{:S(2)}) collective-permute-start(bf16[384,640]{1,0:T(8,128)(2,1)S(1)} %copy-done), channel_id=1, source_target_pairs={{0,24},{8,32},{16,40},{24,48},{32,56},{40,64},{48,72},{56,80},{64,... | collective-permute-start | bytes 1474568 | tf_op jit(solution)/shard_map/ppermute | solution.py:14
  168.6 26.9 %collective-permute-start.7 = (bf16[384,640]{1,0:T(8,128)(2,1)S(1)}, bf16[384,640]{1,0:T(8,128)(2,1)S(1)}, u32[]{:S(2)}, u32[]{:S(2)}) collective-permute-start(bf16[384,640]{1,0:T(8,128)(2,1)S(1)} %copy-done), channel_id=1, source_target_pairs={{0,32},{8,40},{16,48},{24,56},{32,64},{40,72},{48,80},{56,88},{64,... | collective-permute-start | bytes 1474568 | tf_op jit(solution)/shard_map/ppermute | solution.py:14
  170.9 24.8 %copy-start.1 = (bf16[384,640]{1,0:T(8,128)(2,1)S(1)}, bf16[384,640]{1,0:T(8,128)(2,1)}, u32[]{:S(2)}) copy-start(bf16[384,640]{1,0:T(8,128)(2,1)} %param.8) | copy-start | bytes 1474564
Sparse Core Ops, SparseCore 0:
  10.6 113.0 all-gather.1
  222.5 69.0 reduce-scatter.3
where the time goes:
time: 301 us; the launch traced here: 300 us
  blocking collectives  123 us (41%)
  waiting for transfers between devices  94.2 us (31%)
  starting transfers between devices  27.5 us (9%)
  matrix products  17.1 us (6%)
  between operations  17 us (6%)
  local copies, waits for them, and re-layouts  15.4 us (5%)
  other arithmetic  6.31 us (2%)
    all_gather x1, blocking collectives, on_device(): lax.all_gather(text_keys, 'tm', axis=0, tiled=True)  74.3 us
    unnamed x3, waiting for transfers between devices  70 us
    all_gather x1, blocking collectives, on_device(): lax.all_gather(text_values, 'tm', axis=0, tiled=True)  48.6 us
    ppermute x8, starting transfers between devices, from_behind(): lax.ppermute(value, axis, [(source, source + steps) for source in range(i...  27.5 us
    ppermute x8, waiting for transfers between devices, from_behind(): lax.ppermute(value, axis, [(source, source + steps) for source in range(i...  24.2 us
    unnamed x21, local copies, waits for them, and re-layouts  12.2 us
    dot_general x1, matrix products, on_device(): jnp.dot(attended_all, lax.all_gather(out_weight, 'tm', axis=1, tiled=True...  8.94 us
  transfers between devices with their start and end apart: 10, of which 4 were waited for; matrix products, arithmetic and copies ran while one was open for 7% of the time, Pallas kernels for 0%

commit v1 on v0

--- a/solution.py
+++ b/solution.py
@@ -15,13 +15,28 @@
 
 
 def on_device(queries, keys, values, text_keys, text_values, out_weight, windows, lengths):
+
+    def process_sections(inputs, join_dim):
+        chip_axis = "tm"
+        dev_n = lax.axis_size(chip_axis)
+        return lax.all_to_all(
+            jnp.tile(
+                inputs,
+                list(map(lambda dev_i: dev_n if dev_i == join_dim else 1, range(inputs.ndim))),
+            ),
+            chip_axis,
+            concat_axis=join_dim,
+            split_axis=join_dim,
+            tiled=True,
+        )
+
     rows = queries.shape[0]
     width = queries.shape[1]
     local_heads = width // HD
     scale = 1.0 / math.sqrt(HD)
     position = lax.axis_index("tm")
     text_k, text_v = (
-        lax.all_gather(text_keys, "tm", axis=0, tiled=True),
+        process_sections(text_keys, 0),
         lax.all_gather(text_values, "tm", axis=0, tiled=True),
     )
     key_list = [keys]

time: 301 us -> 289 us (0.960)
  blocking collectives: 123 us -> 90.8 us
  local copies, waits for them, and re-layouts: 15.4 us -> 27.9 us
  starting transfers between devices: 27.5 us -> 36.8 us
  waiting for transfers between devices: 94.2 us -> 85.2 us
  matrix products: 17.1 us -> 23.5 us
    all_gather x1 -> x0, blocking collectives: 74.3 us -> none  [on_device(): lax.all_gather(text_keys, 'tm', axis=0, tiled=True)]
    all_gather x1, blocking collectives: 48.6 us -> 90.8 us  [on_device(): lax.all_gather(text_values, 'tm', axis=0, tiled=True)]
    unnamed x21, local copies, waits for them, and re-layouts: 12.2 us -> 21.1 us
    all_to_all x0 -> x1, starting transfers between devices: none -> 8.38 us  [process_sections(): lax.all_to_all(jnp.tile(inputs, list(map(lambda dev_i: dev_n if dev_i ==...]
    ppermute x8, waiting for transfers between devices: 24.2 us -> 16.2 us  [from_behind(): lax.ppermute(value, axis, [(source, source + steps) for source in range(i...]
    dot_general x5, matrix products: 3.71 us -> 9.22 us  [on_device(): jnp.dot(weights.astype(jnp.bfloat16), value_h, preferred_element_type=jnp...]
  transfers between devices with their start and end apart: 10 -> 11, of which waited for: 4 -> 3; matrix products, arithmetic and copies ran while one was open for 7% -> 14% of each run, Pallas kernels for 0% -> 0%
where the time goes in v1:
time: 289 us; the launch traced here: 287 us
  blocking collectives  90.8 us (31%)
  waiting for transfers between devices  85.2 us (29%)
  starting transfers between devices  36.8 us (13%)
  local copies, waits for them, and re-layouts  27.9 us (10%)
  matrix products  23.5 us (8%)
  between operations  16.8 us (6%)
  other arithmetic  6.31 us (2%)
    all_gather x1, blocking collectives, on_device(): lax.all_gather(text_values, 'tm', axis=0, tiled=True)  90.8 us
    unnamed x3, waiting for transfers between devices  69 us
    ppermute x8, starting transfers between devices, from_behind(): lax.ppermute(value, axis, [(source, source + steps) for source in range(i...  28.4 us
    unnamed x21, local copies, waits for them, and re-layouts  21.1 us
    ppermute x8, waiting for transfers between devices, from_behind(): lax.ppermute(value, axis, [(source, source + steps) for source in range(i...  16.2 us
    dot_general x5, matrix products, on_device(): jnp.dot(weights.astype(jnp.bfloat16), value_h, preferred_element_type=jnp...  9.22 us
    dot_general x1, matrix products, on_device(): jnp.dot(attended_all, lax.all_gather(out_weight, 'tm', axis=1, tiled=True...  8.93 us
    all_to_all x1, starting transfers between devices, process_sections(): lax.all_to_all(jnp.tile(inputs, list(map(lambda dev_i: dev_n if dev_i ==...  8.38 us
  transfers between devices with their start and end apart: 11, of which 3 were waited for; matrix products, arithmetic and copies ran while one was open for 14% of the time, Pallas kernels for 0%

profile of v1, /device:TPU:1, one launch (start us, length us, event | category | flops | bytes accessed | tf_op | source)
XLA Modules:
  0.0 287.2 jit_solution(8477077985667173023)
XLA Ops:
  6.5 0.7 all-gather.2.cloned.1.call-update
  7.3 4.5 %collective-permute-start = (bf16[384,640]{1,0:T(8,128)(2,1)}, bf16[384,640]{1,0:T(8,128)(2,1)}, u32[]{:S(2)}, u32[]{:S(2)}) collective-permute-start(bf16[384,640]{1,0:T(8,128)(2,1)} %param.9), channel_id=1, source_target_pairs={{0,8},{8,16},{16,24},{24,32},{32,40},{40,48},{48,56},{56,64},{64,7... | collective-permute-start | bytes 1474568 | tf_op jit(solution)/shard_map/ppermute | solution.py:14
  11.8 3.9 %collective-permute-start.1 = (bf16[384,640]{1,0:T(8,128)(2,1)}, bf16[384,640]{1,0:T(8,128)(2,1)}, u32[]{:S(2)}, u32[]{:S(2)}) collective-permute-start(bf16[384,640]{1,0:T(8,128)(2,1)} %param.9), channel_id=1, source_target_pairs={{0,16},{8,24},{16,32},{24,40},{32,48},{40,56},{48,64},{56,72},{64,... | collective-permute-start | bytes 1474568 | tf_op jit(solution)/shard_map/ppermute | solution.py:14
  15.7 3.5 %collective-permute-start.2 = (bf16[384,640]{1,0:T(8,128)(2,1)}, bf16[384,640]{1,0:T(8,128)(2,1)}, u32[]{:S(2)}, u32[]{:S(2)}) collective-permute-start(bf16[384,640]{1,0:T(8,128)(2,1)} %param.9), channel_id=1, source_target_pairs={{0,24},{8,32},{16,40},{24,48},{32,56},{40,64},{48,72},{56,80},{64,... | collective-permute-start | bytes 1474568 | tf_op jit(solution)/shard_map/ppermute | solution.py:14
  19.2 3.5 %collective-permute-start.3 = (bf16[384,640]{1,0:T(8,128)(2,1)}, bf16[384,640]{1,0:T(8,128)(2,1)}, u32[]{:S(2)}, u32[]{:S(2)}) collective-permute-start(bf16[384,640]{1,0:T(8,128)(2,1)} %param.9), channel_id=1, source_target_pairs={{0,32},{8,40},{16,48},{24,56},{32,64},{40,72},{48,80},{56,88},{64,... | collective-permute-start | bytes 1474568 | tf_op jit(solution)/shard_map/ppermute | solution.py:14
  22.6 1.6 tile.2
  24.3 8.4 %all-to-all-start = ((bf16[64,8,640]{2,1,0:T(8,128)(2,1)}), bf16[64,8,640]{2,1,0:T(8,128)(2,1)}, u32[]{:S(2)}, u32[]{:S(2)}) async-start(bf16[64,8,640]{2,1,0:T(8,128)(2,1)} %tile.2), calls=%async_computation | async-start | bytes 1310720 | tf_op jit(solution)/shard_map/all_to_all | solution.py:22
  32.6 0.0 reduce-scatter.4.cloned.1.call-start
  32.7 3.5 %collective-permute-start.4 = (bf16[384,640]{1,0:T(8,128)(2,1)}, bf16[384,640]{1,0:T(8,128)(2,1)}, u32[]{:S(2)}, u32[]{:S(2)}) collective-permute-start(bf16[384,640]{1,0:T(8,128)(2,1)} %param.10), channel_id=1, source_target_pairs={{0,8},{8,16},{16,24},{24,32},{32,40},{40,48},{48,56},{56,64},{64,7... | collective-permute-start | bytes 1474568 | tf_op jit(solution)/shard_map/ppermute | solution.py:14
  36.3 1.3 dynamic_slice.18
  38.8 1.5 fusion.95
  40.3 0.6 fusion.90
  41.0 1.1 constant_dynamic-update-slice_fusion.4
  42.1 90.8 %all_gather.6 = bf16[512,640]{1,0:T(8,128)(2,1)} all-gather(bf16[8,640]{1,0:T(8,128)(2,1)} %param.12), channel_id=1, replica_groups=mesh['tm'=64,'head'=8] {'tm'}, dimensions={0}, use_global_device_ids=true | all-gather | bytes 665600 | tf_op jit(solution)/shard_map/all_gather | solution.py:40
  132.8 0.6 fusion.91
  134.1 0.6 fusion.92
  135.3 0.6 fusion.93
  136.6 0.7 fusion.94
  137.3 0.3 dynamic-update-slice.17
  137.5 0.2 dynamic-update-slice.18
  137.7 0.2 dynamic-update-slice.19
  137.9 0.2 dynamic-update-slice.20
  138.1 0.2 dynamic-update-slice.21
  138.4 0.2 dynamic-update-slice.22
  138.6 1.9 constant_dynamic-update-slice_fusion.10
  140.5 1.4 collective-permute-start.5
  141.9 1.1 constant_dynamic-update-slice_fusion.3
  143.0 4.8 %collective-permute-start.6 = (bf16[384,640]{1,0:T(8,128)(2,1)}, bf16[384,640]{1,0:T(8,128)(2,1)S(1)}, u32[]{:S(2)}, u32[]{:S(2)}) collective-permute-start(bf16[384,640]{1,0:T(8,128)(2,1)} %param.10), channel_id=1, source_target_pairs={{0,24},{8,32},{16,40},{24,48},{32,56},{40,64},{48,72},{56,80},{64,... | collective-permute-start | bytes 1474568 | tf_op jit(solution)/shard_map/ppermute | solution.py:14
  147.8 1.1 constant_dynamic-update-slice_fusion.2
  148.9 0.0 collective-permute-done.2
  148.9 3.2 %collective-permute-start.7 = (bf16[384,640]{1,0:T(8,128)(2,1)}, bf16[384,640]{1,0:T(8,128)(2,1)S(1)}, u32[]{:S(2)}, u32[]{:S(2)}) collective-permute-start(bf16[384,640]{1,0:T(8,128)(2,1)} %param.10), channel_id=1, source_target_pairs={{0,32},{8,40},{16,48},{24,56},{32,64},{40,72},{48,80},{56,88},{64,... | collective-permute-start | bytes 1474568 | tf_op jit(solution)/shard_map/ppermute | solution.py:14
  152.1 1.1 constant_dynamic-update-slice_fusion.1
  153.2 0.0 collective-permute-done.3
  153.2 1.1 constant_dynamic-update-slice_fusion
  154.3 1.9 constant_dynamic-update-slice_fusion.9
  156.2 0.8 constant_dynamic-update-slice_fusion.8
  157.0 6.5 %collective-permute-done.6 = bf16[384,640]{1,0:T(8,128)(2,1)S(1)} collective-permute-done((bf16[384,640]{1,0:T(8,128)(2,1)}, bf16[384,640]{1,0:T(8,128)(2,1)S(1)}, u32[]{:S(2)}, u32[]{:S(2)}) %collective-permute-start.6) | collective-permute-done | bytes 491552 | tf_op jit(solution)/shard_map/ppermute | solution.py:14
  163.5 0.9 constant_dynamic-update-slice_fusion.7
  164.4 9.7 %collective-permute-done.7 = bf16[384,640]{1,0:T(8,128)(2,1)S(1)} collective-permute-done((bf16[384,640]{1,0:T(8,128)(2,1)}, bf16[384,640]{1,0:T(8,128)(2,1)S(1)}, u32[]{:S(2)}, u32[]{:S(2)}) %collective-permute-start.7) | collective-permute-done | bytes 491552 | tf_op jit(solution)/shard_map/ppermute | solution.py:14
  174.0 0.9 constant_dynamic-update-slice_fusion.6
  174.9 1.0 constant_dynamic-update-slice_fusion.5
  175.9 1.2 bitcast_dynamic-update-slice_fusion
  177.0 0.0 copy-start.1
  177.1 1.8 fusion.96
  178.9 0.6 fusion.5
  179.5 0.9 fusion.97
  180.4 0.6 fusion.7
  181.0 0.9 fusion.98
  181.9 0.6 fusion.9
  182.5 0.9 fusion.99
  183.4 0.6 fusion.11
  184.0 0.9 fusion.100
  184.9 0.6 fusion.13
  185.5 1.9 fusion.72
  187.4 1.8 fusion.66
  189.2 1.8 fusion.60
  191.1 1.8 fusion.54
  192.9 1.8 fusion.48
  194.8 0.0 all-gather.2.cloned.1.call-done
  194.8 8.9 %convolution_convert_fusion = bf16[384,5120]{1,0:T(8,128)(2,1)} fusion(bf16[384,640]{1,0:T(8,128)(2,1)S(1)} %fusion.48, bf16[640,5120]{0,1:T(8,128)(2,1)} %all-gather.2.cloned.1.call-done), kind=kOutput, calls=%fused_computation | convolution fusion | flops 2518548480 | bytes 10977280 | tf_op jit(solution)/shard_map/dot_general | solution.py:82
  203.8 6.3 %copy.9 = bf16[384,5120]{0,1:T(8,128)(2,1)} copy(bf16[384,5120]{1,0:T(8,128)(2,1)} %convolution_convert_fusion) | data formatting | bytes 7864320
  210.0 0.0 reduce-scatter.4.cloned.1.call-update
  210.0 68.3 %reduce-scatter.4.cloned.1.call-done = bf16[640,384]{1,0:T(8,128)(2,1)} async-done(((bf16[5120,384]{1,0:T(8,128)(2,1)}), bf16[640,384]{1,0:T(8,128)(2,1)}) %reduce-scatter.4.cloned.1.call-update) | async-done | bytes 491536
  278.4 2.0 copy.10
  (11 shorter events, 0.0 us)
Async XLA Ops:
  6.5 188.3 %all-gather.2.cloned.1.call-start = ((), (), s32[]{:S(2)}) async-start(), calls=%async_computation.2 | async-start | bytes 6656000 | tf_op jit(solution)/shard_map/all_gather | solution.py:84
  7.3 133.2 %collective-permute-start = (bf16[384,640]{1,0:T(8,128)(2,1)}, bf16[384,640]{1,0:T(8,128)(2,1)}, u32[]{:S(2)}, u32[]{:S(2)}) collective-permute-start(bf16[384,640]{1,0:T(8,128)(2,1)} %param.9), channel_id=1, source_target_pairs={{0,8},{8,16},{16,24},{24,32},{32,40},{40,48},{48,56},{56,64},{64,7... | collective-permute-start | bytes 1474568 | tf_op jit(solution)/shard_map/ppermute | solution.py:14
  11.8 131.2 %collective-permute-start.1 = (bf16[384,640]{1,0:T(8,128)(2,1)}, bf16[384,640]{1,0:T(8,128)(2,1)}, u32[]{:S(2)}, u32[]{:S(2)}) collective-permute-start(bf16[384,640]{1,0:T(8,128)(2,1)} %param.9), channel_id=1, source_target_pairs={{0,16},{8,24},{16,32},{24,40},{32,48},{40,56},{48,64},{56,72},{64,... | collective-permute-start | bytes 1474568 | tf_op jit(solution)/shard_map/ppermute | solution.py:14
  15.7 133.2 %collective-permute-start.2 = (bf16[384,640]{1,0:T(8,128)(2,1)}, bf16[384,640]{1,0:T(8,128)(2,1)}, u32[]{:S(2)}, u32[]{:S(2)}) collective-permute-start(bf16[384,640]{1,0:T(8,128)(2,1)} %param.9), channel_id=1, source_target_pairs={{0,24},{8,32},{16,40},{24,48},{32,56},{40,64},{48,72},{56,80},{64,... | collective-permute-start | bytes 1474568 | tf_op jit(solution)/shard_map/ppermute | solution.py:14
  19.2 134.1 %collective-permute-start.3 = (bf16[384,640]{1,0:T(8,128)(2,1)}, bf16[384,640]{1,0:T(8,128)(2,1)}, u32[]{:S(2)}, u32[]{:S(2)}) collective-permute-start(bf16[384,640]{1,0:T(8,128)(2,1)} %param.9), channel_id=1, source_target_pairs={{0,32},{8,40},{16,48},{24,56},{32,64},{40,72},{48,80},{56,88},{64,... | collective-permute-start | bytes 1474568 | tf_op jit(solution)/shard_map/ppermute | solution.py:14
  24.3 151.6 %all-to-all-start = ((bf16[64,8,640]{2,1,0:T(8,128)(2,1)}), bf16[64,8,640]{2,1,0:T(8,128)(2,1)}, u32[]{:S(2)}, u32[]{:S(2)}) async-start(bf16[64,8,640]{2,1,0:T(8,128)(2,1)} %tile.2), calls=%async_computation | async-start | bytes 1310720 | tf_op jit(solution)/shard_map/all_to_all | solution.py:22
  32.6 245.7 %reduce-scatter.4.cloned.1.call-start = ((), (), s32[]{:S(2)}) async-start(), calls=%async_computation.3 | async-start | bytes 4423680
  32.7 121.6 %collective-permute-start.4 = (bf16[384,640]{1,0:T(8,128)(2,1)}, bf16[384,640]{1,0:T(8,128)(2,1)}, u32[]{:S(2)}, u32[]{:S(2)}) collective-permute-start(bf16[384,640]{1,0:T(8,128)(2,1)} %param.10), channel_id=1, source_target_pairs={{0,8},{8,16},{16,24},{24,32},{32,40},{40,48},{48,56},{56,64},{64,7... | collective-permute-start | bytes 1474568 | tf_op jit(solution)/shard_map/ppermute | solution.py:14
  140.5 34.4 %copy-start = (bf16[512,640]{1,0:T(8,128)(2,1)S(1)}, bf16[512,640]{1,0:T(8,128)(2,1)}, u32[]{:S(2)}) copy-start(bf16[512,640]{1,0:T(8,128)(2,1)} %all_gather.6) | copy-start | bytes 1966084
  140.5 15.7 %collective-permute-start.5 = (bf16[384,640]{1,0:T(8,128)(2,1)}, bf16[384,640]{1,0:T(8,128)(2,1)S(1)}, u32[]{:S(2)}, u32[]{:S(2)}) collective-permute-start(bf16[384,640]{1,0:T(8,128)(2,1)} %param.10), channel_id=1, source_target_pairs={{0,16},{8,24},{16,32},{24,40},{32,48},{40,56},{48,64},{56,72},{64,... | collective-permute-start | bytes 1474568 | tf_op jit(solution)/shard_map/ppermute | solution.py:14
  143.0 20.5 %collective-permute-start.6 = (bf16[384,640]{1,0:T(8,128)(2,1)}, bf16[384,640]{1,0:T(8,128)(2,1)S(1)}, u32[]{:S(2)}, u32[]{:S(2)}) collective-permute-start(bf16[384,640]{1,0:T(8,128)(2,1)} %param.10), channel_id=1, source_target_pairs={{0,24},{8,32},{16,40},{24,48},{32,56},{40,64},{48,72},{56,80},{64,... | collective-permute-start | bytes 1474568 | tf_op jit(solution)/shard_map/ppermute | solution.py:14
  148.9 25.1 %collective-permute-start.7 = (bf16[384,640]{1,0:T(8,128)(2,1)}, bf16[384,640]{1,0:T(8,128)(2,1)S(1)}, u32[]{:S(2)}, u32[]{:S(2)}) collective-permute-start(bf16[384,640]{1,0:T(8,128)(2,1)} %param.10), channel_id=1, source_target_pairs={{0,32},{8,40},{16,48},{24,56},{32,64},{40,72},{48,80},{56,88},{64,... | collective-permute-start | bytes 1474568 | tf_op jit(solution)/shard_map/ppermute | solution.py:14
  177.0 2.5 copy-start.1
Sparse Core Ops, SparseCore 0:
  10.6 115.6 all-gather.1
  210.2 68.1 reduce-scatter.3
